TPU v7x, 512 devices: a whole 4x4x16 slice. The times are simulated.
512 devices in a mesh: gx: 8 (over x, core), gy: 4 (over y), gz: 16 (over z).
Axes of the slice: x: 4, y: 4, z: 16, core: 2. Of those that a mesh axis runs over, the one named last changes fastest.
Arguments:
- multipoles: bfloat16 [289, 262144], P(None, ('gx', 'gy', 'gz')), may hold values from -6 to 6
- up_shift: bfloat16 [8, 289, 289], replicated, may hold values from -0.125 to 0.125
- down_shift: bfloat16 [8, 289, 289], replicated, may hold values from -0.375 to 0.375
- far_shift: bfloat16 [8, 289, 289], replicated, may hold values from -0.09375 to 0.09375
- send_list: int32 [8, 64, 64, 16], P('gx', ('gy', 'gz')), may hold values from 0 to 511
- leaf_src: int32 [16, 262144], P(None, ('gx', 'gy', 'gz')), may hold values from 0 to 1535
- leaf_kind: int32 [16, 262144], P(None, ('gx', 'gy', 'gz')), may hold values from 0 to 7
- coarse_src: int32 [8, 64], replicated, may hold values from 0 to 63
- coarse_kind: int32 [8, 64], replicated, may hold values from 0 to 7
Outputs:
- leaf_local: bfloat16 [289, 262144], P(None, ('gx', 'gy', 'gz'))
All inputs are finite; a program needn't handle non-finite values.
Results may differ from a plain program's by a relative error of at most 0.014.
Values may be sent and summed in bfloat16 or wider, within the bound.
No kernel may reach another device: no remote copies, remote signals or barrier semaphores. Data moves between devices by JAX's collectives and lax.ppermute only.
A program may use at most 128 MiB of HBM per device.

v0:
```python
import jax
import jax.numpy as jnp
from jax import lax
from jax.sharding import PartitionSpec as P

LOCAL_LEVELS = 3


def lift_level(children, up_shift):
    coefs = children.shape[0]
    count = children.shape[1] // 8
    child_stack = children.reshape(coefs, count, 8).transpose(2, 0, 1).reshape(8 * coefs, count)
    shift_table = up_shift.transpose(1, 0, 2).reshape(coefs, 8 * coefs)
    return jnp.dot(shift_table, child_stack, preferred_element_type=jnp.float32)


def lower_level(parent, down_shift):
    coefs = parent.shape[0]
    count = parent.shape[1]
    spread = jnp.dot(
        down_shift.reshape(8 * coefs, coefs), parent, preferred_element_type=jnp.float32
    )
    return spread.reshape(8, coefs, count).transpose(1, 2, 0).reshape(coefs, 8 * count)


def on_device(
    multipoles,
    up_shift,
    down_shift,
    far_shift,
    send_list,
    leaf_src,
    leaf_kind,
    coarse_src,
    coarse_kind,
):
    coefs = multipoles.shape[0]
    kind_count = far_shift.shape[0]
    flat_index = lax.axis_index(("gx", "gy", "gz"))
    coarse_box = flat_index // 8
    octant = flat_index % 8
    peer_count = lax.axis_size(("gy", "gz"))
    slot_count = send_list.shape[3]
    send_order = send_list.reshape(peer_count * slot_count)
    outgoing = jnp.take(multipoles, send_order, axis=1)
    arrived = lax.all_to_all(outgoing, ("gy", "gz"), split_axis=1, concat_axis=1, tiled=True)
    upward = multipoles
    for level in range(LOCAL_LEVELS):
        upward = lift_level(upward, up_shift).astype(jnp.bfloat16)
    every_box = lax.all_gather(upward, ("gx", "gy", "gz"), axis=1, tiled=True)
    coarse_multi = lift_level(every_box, up_shift).astype(jnp.bfloat16)
    coarse_cols = coarse_src[:, coarse_box]
    coarse_kinds = coarse_kind[:, coarse_box]
    list_len = coarse_cols.shape[0]
    coarse_picked = jnp.take(coarse_multi, coarse_cols, axis=1)
    stacked = (
        jnp.take(far_shift, coarse_kinds, axis=0)
        .transpose(1, 0, 2)
        .reshape(coefs, list_len * coefs)
    )
    column_vec = coarse_picked.transpose(1, 0).reshape(list_len * coefs, 1)
    coarse_local = jnp.dot(stacked, column_vec, preferred_element_type=jnp.float32).astype(
        jnp.bfloat16
    )
    downward = jnp.dot(down_shift[octant], coarse_local, preferred_element_type=jnp.float32).astype(
        jnp.bfloat16
    )
    for level in range(LOCAL_LEVELS - 1):
        downward = lower_level(downward, down_shift).astype(jnp.bfloat16)
    chain_part = lower_level(downward, down_shift)
    buffer = jnp.concatenate([multipoles, arrived], axis=1)
    leaf_count = leaf_src.shape[1]
    picked = jnp.take(buffer, leaf_src, axis=1)
    kind_range = jnp.arange(kind_count, dtype=jnp.int32)
    kind_hot = (leaf_kind[None, :, :] == kind_range[:, None, None]).astype(jnp.bfloat16)
    grouped = jnp.einsum("plt,klt->kpt", picked, kind_hot, preferred_element_type=jnp.float32)
    grouped = grouped.reshape(kind_count * coefs, leaf_count)
    upper_part = grouped.astype(jnp.bfloat16)
    lower_part = (grouped - upper_part.astype(jnp.float32)).astype(jnp.bfloat16)
    shift_table = far_shift.transpose(1, 0, 2).reshape(coefs, kind_count * coefs)
    far_total = jnp.dot(shift_table, upper_part, preferred_element_type=jnp.float32)
    far_total = far_total + jnp.dot(shift_table, lower_part, preferred_element_type=jnp.float32)
    return (chain_part + far_total).astype(jnp.bfloat16)


def solution(mesh):
    in_specs = (
        P(None, ("gx", "gy", "gz")),
        P(),
        P(),
        P(),
        P("gx", ("gy", "gz"), None, None),
        P(None, ("gx", "gy", "gz")),
        P(None, ("gx", "gy", "gz")),
        P(),
        P(),
    )
    out_specs = P(None, ("gx", "gy", "gz"))
    return jax.shard_map(
        on_device, mesh=mesh, in_specs=in_specs, out_specs=out_specs, check_vma=False
    )
```

profile of v0, /device:TPU:32, one launch (start us, length us, event | category | flops | bytes accessed | tf_op | source)
XLA Modules:
  0.0 275.0 jit_solution(4691575993083344755)
XLA Ops:
  0.0 0.8 copy.104
  0.8 0.7 compare_and_fusion.1
  1.5 1.2 copy.91
  2.9 3.9 %gather_fusion.2 = bf16[1024,289]{1,0:T(8,128)(2,1)S(1)} fusion(bf16[289,512]{0,1:T(8,128)(2,1)S(1)} %copy.91, s32[1024]{0:T(1024)S(1)} %broadcast_clamp_fusion.1), kind=kCustom, calls=%fused_computation.2 | custom fusion | bytes 1187840 | tf_op jit(solution)/shard_map/jit(_take)/gather | solution.py:45
  6.8 1.1 broadcast_select_fusion
  7.9 18.4 %all-to-all-start = ((bf16[289,64,16]{0,2,1:T(8,128)(2,1)}), bf16[289,64,16]{0,2,1:T(8,128)(2,1)S(1)}, u32[]{:S(2)}, u32[]{:S(2)}) async-start(bf16[289,64,16]{0,2,1:T(8,128)(2,1)} %broadcast_select_fusion), calls=%async_computation | async-start | bytes 1572864 | tf_op jit(solution)/shard_map/all_to_all | solution.py:46
  26.5 0.2 and_reduce_fusion
  27.0 3.0 %reshape.137 = bf16[289,2312]{1,0:T(8,128)(2,1)} reshape(bf16[289,8,289]{2,1,0:T(8,128)(2,1)S(1)} %bitcast.160) | data formatting | bytes 2672672 | tf_op jit(solution)/shard_map/reshape | solution.py:13
  29.9 0.7 fusion.45
  30.7 0.6 fusion.57
  31.4 2.0 convolution_reduce_fusion.1
  33.4 151.1 %all-gather = bf16[512,1,289]{2,1,0:T(2,128)(2,1)S(1)} all-gather(bf16[1,1,289]{2,1,0:T(2,128)(2,1)S(1)} %reshape.178), channel_id=1, replica_groups=mesh['gx'=8,'gy'=4,'gz'=16] {'gx','gy','gz'}, dimensions={0}, use_global_device_ids=true | all-gather | bytes 296514 | tf_op jit(solution)/shard_map/all_gather | solution.py:50
  184.6 0.7 fusion.48
  185.4 0.6 gather_fusion.1
  186.1 6.8 %gather_fusion = bf16[8,289,289]{2,0,1:T(8,128)(2,1)} fusion(bf16[8,289,289]{2,0,1:T(8,128)(2,1)S(1)} %copy-done, s32[1024]{0:T(1024)S(1)} %pad_clamp_fusion.1), kind=kCustom, calls=%fused_computation | custom fusion | bytes 2672704 | tf_op jit(solution)/shard_map/jit(_take)/gather | solution.py:57
  192.9 1.8 select_bitcast_fusion
  194.7 0.6 fusion.60
  195.3 4.5 %copy.100 = bf16[8,289,289]{1,0,2:T(8,128)(2,1)} copy(bf16[8,289,289]{2,0,1:T(8,128)(2,1)} %param.11) | data formatting | bytes 2672672 | tf_op args[2]
  199.8 1.9 constant_dynamic-slice_fusion
  202.0 4.1 %reshape.139 = bf16[2312,289]{0,1:T(8,128)(2,1)} reshape(bf16[8,289,289]{1,0,2:T(8,128)(2,1)} %copy.100) | data formatting | bytes 2672672 | tf_op jit(solution)/shard_map/reshape | solution.py:21
  206.0 2.3 fusion.8
  208.3 0.3 fusion.4
  208.8 2.6 convolution_bitcast_fusion
  211.4 2.4 reshape.140
  213.8 2.2 copy.113
  216.4 3.2 %copy.119 = bf16[289,8,289]{0,1,2:T(8,128)(2,1)} copy(bf16[289,8,289]{2,1,0:T(8,128)(2,1)S(1)} %bitcast.158) | data formatting | bytes 2672672 | tf_op jit(solution)/shard_map/transpose | solution.py:80
  219.7 33.2 %gather_fusion.3 = bf16[8192,289]{1,0:T(8,128)(2,1)} fusion(bf16[289,1536]{0,1:T(8,128)(2,1)S(1)} %pad_maximum_fusion, s32[8192]{0:T(1024)S(1)} %broadcast_clamp_fusion), kind=kCustom, calls=%fused_computation.3 | custom fusion | bytes 9502720 | tf_op jit(solution)/shard_map/jit(_take)/gather | solution.py:73
  252.9 10.0 %fusion = f32[512,8,289]{2,1,0:T(8,128)} fusion(bf16[16,512,289]{2,1,0:T(8,128)(2,1)} %bitcast.164, pred[16,512]{0,1:T(8,128)(4,1)S(1)} %copy.102, s32[16,512]{0,1:T(8,128)S(1)} %copy.101), kind=kOutput, calls=%fused_computation.4 | convolution fusion | flops 40312832 | bytes 9510912 | tf_op jit(solution)/shard_map/plt,klt->kpt/dot_general | solution.py:76
  262.8 6.5 %copy.108 = f32[512,8,289]{0,1,2:T(8,128)} copy(f32[512,8,289]{2,1,0:T(8,128)} %fusion) | data formatting | bytes 9469952 | tf_op jit(solution)/shard_map/plt,klt->kpt/dot_general | solution.py:76
  269.3 3.5 %convolution_bitcast_fusion.1 = f32[512,289]{0,1:T(8,128)S(1)} fusion(bf16[289,8,289]{0,1,2:T(8,128)(2,1)S(1)} %copy-done.5, f32[512,8,289]{0,1,2:T(8,128)} %copy.108), kind=kOutput, calls=%fused_computation.29 | convolution fusion | flops 684204032 | bytes 6663184 | tf_op jit(solution)/shard_map/dot_general | solution.py:81
  272.9 0.2 copy-done.1
  273.2 1.7 fusion.30
  (45 shorter events, 1.9 us)
Async XLA Ops:
  6.8 19.5 %copy-start.9 = (s32[8,64]{1,0:T(8,128)S(1)}, s32[8,64]{1,0:T(8,128)}, u32[]{:S(2)}) copy-start(s32[8,64]{1,0:T(8,128)} %param.17) | copy-start | bytes 6148
  6.8 19.7 %copy-start.10 = (s32[8,64]{1,0:T(8,128)S(1)}, s32[8,64]{1,0:T(8,128)}, u32[]{:S(2)}) copy-start(s32[8,64]{1,0:T(8,128)} %param.16) | copy-start | bytes 6148
  6.8 20.2 %copy-start.3 = (bf16[8,289,289]{2,0,1:T(8,128)(2,1)S(1)}, bf16[8,289,289]{2,0,1:T(8,128)(2,1)}, u32[]{:S(2)}) copy-start(bf16[8,289,289]{2,0,1:T(8,128)(2,1)} %param.10) | copy-start | bytes 4009012
  7.9 211.6 %all-to-all-start = ((bf16[289,64,16]{0,2,1:T(8,128)(2,1)}), bf16[289,64,16]{0,2,1:T(8,128)(2,1)S(1)}, u32[]{:S(2)}, u32[]{:S(2)}) async-start(bf16[289,64,16]{0,2,1:T(8,128)(2,1)} %broadcast_select_fusion), calls=%async_computation | async-start | bytes 1572864 | tf_op jit(solution)/shard_map/all_to_all | solution.py:46
  31.4 153.2 %copy-start.4 = (bf16[8,289,289]{2,0,1:T(8,128)(2,1)S(1)}, bf16[8,289,289]{2,0,1:T(8,128)(2,1)}, u32[]{:S(2)}) copy-start(bf16[8,289,289]{2,0,1:T(8,128)(2,1)} %param.10) | copy-start | bytes 4009012
  184.6 1.5 copy-start
  206.0 2.3 copy-start.2
  211.4 4.6 %copy-start.7 = (s32[16,512]{1,0:T(8,128)S(1)}, s32[16,512]{1,0:T(8,128)}, u32[]{:S(2)}) copy-start(s32[16,512]{1,0:T(8,128)} %param.14) | copy-start | bytes 98308
  211.4 4.6 %copy-start.8 = (s32[16,512]{1,0:T(8,128)S(1)}, s32[16,512]{1,0:T(8,128)}, u32[]{:S(2)}) copy-start(s32[16,512]{1,0:T(8,128)} %param.15) | copy-start | bytes 98308
  262.8 6.5 %copy-start.5 = (bf16[289,8,289]{0,1,2:T(8,128)(2,1)S(1)}, bf16[289,8,289]{0,1,2:T(8,128)(2,1)}, u32[]{:S(2)}) copy-start(bf16[289,8,289]{0,1,2:T(8,128)(2,1)} %copy.119) | copy-start | bytes 4009012
  269.3 3.8 %copy-start.1 = (f32[512,8,289]{0,1,2:T(8,128)S(1)}, f32[512,8,289]{0,1,2:T(8,128)}, u32[]{:S(2)}) copy-start(f32[512,8,289]{0,1,2:T(8,128)} %copy.108) | copy-start | bytes 14204932
  269.3 3.9 %copy-start.6 = (f32[289,512]{1,0:T(8,128)S(1)}, f32[289,512]{1,0:T(8,128)}, u32[]{:S(2)}) copy-start(f32[289,512]{1,0:T(8,128)} %copy.113) | copy-start | bytes 1775620
where the time goes:
time: 276 us; the launch traced here: 275 us
  blocking collectives  151 us (55%)
  local copies, waits for them, and re-layouts  75.5 us (27%)
  matrix products  25.2 us (9%)
  starting transfers between devices  18.4 us (7%)
  other arithmetic  4.45 us (2%)
    all_gather x1, blocking collectives, on_device(): every_box = lax.all_gather(upward, ('gx', 'gy', 'gz'), axis=1, tiled=True)  151 us
    gather x1, local copies, waits for them, and re-layouts, on_device(): picked = jnp.take(buffer, leaf_src, axis=1)  33.2 us
    all_to_all x1, starting transfers between devices, on_device(): lax.all_to_all(outgoing, ('gy', 'gz'), split_axis=1, concat_axis=1, tiled...  18.4 us
    dot_general x1, matrix products, on_device(): jnp.einsum('plt,klt->kpt', picked, kind_hot, preferred_element_type=jnp.f...  9.96 us
    unnamed x29, local copies, waits for them, and re-layouts  7.11 us
    gather x1, local copies, waits for them, and re-layouts, on_device(): jnp.take(far_shift, coarse_kinds, axis=0).transpose(1, 0, 2)  6.81 us
    dot_general x1, local copies, waits for them, and re-layouts, on_device(): jnp.einsum('plt,klt->kpt', picked, kind_hot, preferred_element_type=jnp.f...  6.5 us
  transfers between devices with their start and end apart: 1, of which 0 were waited for; matrix products, arithmetic and copies ran while one was open for 15% of the time, Pallas kernels for 0%

commit v1 on v0

--- a/solution.py
+++ b/solution.py
@@ -47,7 +47,12 @@
     upward = multipoles
     for level in range(LOCAL_LEVELS):
         upward = lift_level(upward, up_shift).astype(jnp.bfloat16)
-    every_box = lax.all_gather(upward, ("gx", "gy", "gz"), axis=1, tiled=True)
+    every_box = jnp.concatenate(
+        lax.all_to_all(
+            jnp.stack([upward] * lax.axis_size(("gx", "gy", "gz"))), ("gx", "gy", "gz"), 0, 0
+        ),
+        axis=1,
+    )
     coarse_multi = lift_level(every_box, up_shift).astype(jnp.bfloat16)
     coarse_cols = coarse_src[:, coarse_box]
     coarse_kinds = coarse_kind[:, coarse_box]

time: 276 us -> 185 us (0.67)
  the two profiles are of different devices: /device:TPU:32 before, /device:TPU:10 now
where the time goes in v1:
time: 185 us; the launch traced here: 184 us
  local copies, waits for them, and re-layouts  73.8 us (40%)
  waiting for transfers between devices  50.4 us (27%)
  starting transfers between devices  29.6 us (16%)
  matrix products  22.9 us (12%)
  other arithmetic  7.35 us (4%)
    all_to_all x1, waiting for transfers between devices, on_device(): lax.all_to_all(jnp.stack([upward] * lax.axis_size(('gx', 'gy', 'gz'))), (...  37 us
    gather x1, local copies, waits for them, and re-layouts, on_device(): picked = jnp.take(buffer, leaf_src, axis=1)  33.2 us
    all_to_all x1, starting transfers between devices, on_device(): lax.all_to_all(jnp.stack([upward] * lax.axis_size(('gx', 'gy', 'gz'))), (...  23.2 us
    all_to_all x1, waiting for transfers between devices, on_device(): lax.all_to_all(outgoing, ('gy', 'gz'), split_axis=1, concat_axis=1, tiled...  13.4 us
    dot_general x1, matrix products, on_device(): jnp.einsum('plt,klt->kpt', picked, kind_hot, preferred_element_type=jnp.f...  9.96 us
    gather x1, local copies, waits for them, and re-layouts, on_device(): jnp.take(far_shift, coarse_kinds, axis=0).transpose(1, 0, 2)  6.81 us
    dot_general x1, local copies, waits for them, and re-layouts, on_device(): jnp.einsum('plt,klt->kpt', picked, kind_hot, preferred_element_type=jnp.f...  6.5 us
    all_to_all x1, starting transfers between devices, on_device(): lax.all_to_all(outgoing, ('gy', 'gz'), split_axis=1, concat_axis=1, tiled...  6.35 us
  transfers between devices with their start and end apart: 2, of which 2 were waited for; matrix products, arithmetic and copies ran while one was open for 20% of the time, Pallas kernels for 0%

profile of v1, /device:TPU:10, one launch (start us, length us, event | category | flops | bytes accessed | tf_op | source)
XLA Modules:
  0.0 184.4 jit_solution(4358910705173916672)
XLA Ops:
  0.0 1.2 copy.67
  1.2 4.2 %reshape.140 = bf16[289,2312]{1,0:T(8,128)(2,1)} reshape(bf16[289,8,289]{2,1,0:T(8,128)(2,1)} %bitcast.158) | data formatting | bytes 2672672 | tf_op jit(solution)/shard_map/reshape | solution.py:13
  5.4 0.7 fusion.45
  6.1 0.6 fusion.57
  6.9 1.9 %convolution_reduce_fusion.1 = bf16[289]{0:T(512)(128)(2,1)S(1)} fusion(bf16[2312,1]{0,1:T(2,128)(2,1)S(1)} %reshape.183, bf16[289,2312]{1,0:T(8,128)(2,1)} %reshape.140), kind=kOutput, calls=%fused_computation.46 | convolution fusion | flops 1336336 | bytes 1341538 | tf_op jit(solution)/shard_map/dot_general | solution.py:14
  8.7 1.3 stack.2
  10.0 23.2 %all-to-all-start = ((bf16[512,289,1]{1,2,0:T(2,128)(2,1)}), bf16[512,289,1]{1,2,0:T(2,128)(2,1)S(1)}, u32[]{:S(2)}, u32[]{:S(2)}) async-start(bf16[512,289,1]{1,2,0:T(2,128)(2,1)} %stack.2), calls=%async_computation | async-start | bytes 1572864 | tf_op jit(solution)/shard_map/all_to_all | solution.py:51
  33.5 5.0 %gather_fusion.2 = bf16[1024,289]{1,0:T(8,128)(2,1)} fusion(bf16[289,512]{0,1:T(8,128)(2,1)S(1)} %copy.67, s32[1024]{0:T(1024)S(1)} %broadcast_clamp_fusion.1), kind=kCustom, calls=%fused_computation.2 | custom fusion | bytes 1187840 | tf_op jit(solution)/shard_map/jit(_take)/gather | solution.py:45
  39.1 2.2 %broadcast_select_fusion = bf16[289,64,16]{0,2,1:T(8,128)(2,1)} fusion(bf16[289,64,16]{0,2,1:T(8,128)(2,1)} %bitcast.164, pred[64,16]{1,0:T(8,128)(4,1)S(1)} %copy.78), kind=kLoop, calls=%fused_computation.48 | loop fusion | flops 295936 | bytes 1184768 | tf_op jit(solution)/shard_map/jit(_take)/select_n | solution.py:45
  41.3 37.0 %all-to-all-done = bf16[512,289,1]{1,2,0:T(2,128)(2,1)S(1)} async-done(((bf16[512,289,1]{1,2,0:T(2,128)(2,1)}), bf16[512,289,1]{1,2,0:T(2,128)(2,1)S(1)}, u32[]{:S(2)}, u32[]{:S(2)}) %all-to-all-start) | async-done | bytes 295968 | tf_op jit(solution)/shard_map/all_to_all | solution.py:51
  78.3 6.3 %all-to-all-start.1 = ((bf16[289,64,16]{0,2,1:T(8,128)(2,1)}), bf16[289,64,16]{0,2,1:T(8,128)(2,1)}, u32[]{:S(2)}, u32[]{:S(2)}) async-start(bf16[289,64,16]{0,2,1:T(8,128)(2,1)} %broadcast_select_fusion), calls=%async_computation.1 | async-start | bytes 1572864 | tf_op jit(solution)/shard_map/all_to_all | solution.py:46
  84.7 3.1 %copy.75 = bf16[8,289,289]{1,0,2:T(8,128)(2,1)} copy(bf16[8,289,289]{2,0,1:T(8,128)(2,1)S(1)} %copy-done.3) | data formatting | bytes 2672672 | tf_op args[2]
  87.9 4.2 %reshape.142 = bf16[2312,289]{0,1:T(8,128)(2,1)} reshape(bf16[8,289,289]{1,0,2:T(8,128)(2,1)} %copy.75) | data formatting | bytes 2672672 | tf_op jit(solution)/shard_map/reshape | solution.py:21
  92.1 0.8 copy.76
  93.1 6.8 %gather_fusion = bf16[8,289,289]{2,0,1:T(8,128)(2,1)} fusion(bf16[8,289,289]{2,0,1:T(8,128)(2,1)S(1)} %copy-done, s32[1024]{0:T(1024)S(1)} %pad_clamp_fusion.1), kind=kCustom, calls=%fused_computation | custom fusion | bytes 2672704 | tf_op jit(solution)/shard_map/jit(_take)/gather | solution.py:62
  99.9 3.2 %copy.94 = bf16[289,8,289]{0,1,2:T(8,128)(2,1)} copy(bf16[289,8,289]{2,1,0:T(8,128)(2,1)S(1)} %bitcast.156) | data formatting | bytes 2672672 | tf_op jit(solution)/shard_map/transpose | solution.py:85
  103.3 1.9 %constant_dynamic-slice_fusion = bf16[1,289,289]{2,0,1:T(2,128)(2,1)S(1)} fusion(bf16[8,289,289]{2,0,1:T(8,128)(2,1)} %param.11, s32[]{:T(128)S(6)} %select_n.79), kind=kLoop, calls=%fused_computation.77 | loop fusion | bytes 334088 | tf_op jit(solution)/shard_map/dynamic_slice | solution.py:70
  105.3 3.1 %select_bitcast_fusion = bf16[289,8,289]{2,1,0:T(8,128)(2,1)} fusion(bf16[8,289,289]{2,0,1:T(8,128)(2,1)} %gather_fusion, pred[8]{0:T(512)(128)(4,1)S(1)} %get-tuple-element.6), kind=kLoop, calls=%fused_computation.21 | loop fusion | flops 668168 | bytes 2672680 | tf_op jit(solution)/shard_map/jit(_take)/select_n | solution.py:62
  108.5 0.7 fusion.48
  109.2 0.6 gather_fusion.1
  109.9 2.2 %fusion.60 = bf16[289]{0:T(512)(128)(2,1)S(1)} fusion(bf16[289,8,289]{2,1,0:T(8,128)(2,1)} %select_bitcast_fusion, bf16[8,289,1]{1,0,2:T(8,128)(2,1)S(1)} %select_bitcast_fusion.1), kind=kOutput, calls=%fused_computation.44 | convolution fusion | flops 1336336 | bytes 1341538 | tf_op jit(solution)/shard_map/dot_general | solution.py:67
  112.4 0.7 fusion.8
  113.1 0.3 fusion.4
  113.6 0.4 convolution_bitcast_fusion
  113.9 0.4 reshape.143
  114.6 13.4 %all-to-all-done.1 = bf16[289,64,16]{0,2,1:T(8,128)(2,1)} async-done(((bf16[289,64,16]{0,2,1:T(8,128)(2,1)}), bf16[289,64,16]{0,2,1:T(8,128)(2,1)}, u32[]{:S(2)}, u32[]{:S(2)}) %all-to-all-start.1) | async-done | bytes 591904 | tf_op jit(solution)/shard_map/all_to_all | solution.py:46
  128.0 1.3 pad_maximum_fusion
  129.3 33.2 %gather_fusion.3 = bf16[8192,289]{1,0:T(8,128)(2,1)} fusion(bf16[289,1536]{0,1:T(8,128)(2,1)S(1)} %pad_maximum_fusion, s32[8192]{0:T(1024)S(1)} %broadcast_clamp_fusion), kind=kCustom, calls=%fused_computation.3 | custom fusion | bytes 9502720 | tf_op jit(solution)/shard_map/jit(_take)/gather | solution.py:78
  162.5 10.0 %fusion = f32[512,8,289]{2,1,0:T(8,128)} fusion(bf16[16,512,289]{2,1,0:T(8,128)(2,1)} %bitcast.162, pred[16,512]{0,1:T(8,128)(4,1)S(1)} %copy.77, s32[16,512]{0,1:T(8,128)S(1)} %copy-done.8), kind=kOutput, calls=%fused_computation.4 | convolution fusion | flops 40312832 | bytes 9510912 | tf_op jit(solution)/shard_map/plt,klt->kpt/dot_general | solution.py:81
  172.5 6.5 %copy.83 = f32[512,8,289]{0,1,2:T(8,128)} copy(f32[512,8,289]{2,1,0:T(8,128)} %fusion) | data formatting | bytes 9469952 | tf_op jit(solution)/shard_map/plt,klt->kpt/dot_general | solution.py:81
  179.0 3.5 %convolution_bitcast_fusion.1 = f32[512,289]{0,1:T(8,128)S(1)} fusion(bf16[289,8,289]{0,1,2:T(8,128)(2,1)S(1)} %copy-done.7, f32[512,8,289]{0,1,2:T(8,128)} %copy.83), kind=kOutput, calls=%fused_computation.29 | convolution fusion | flops 684204032 | bytes 6663184 | tf_op jit(solution)/shard_map/dot_general | solution.py:86
  182.7 1.7 fusion.30
  (52 shorter events, 2.2 us)
Async XLA Ops:
  1.2 4.2 %copy-start.5 = (bf16[8,289,289]{2,0,1:T(8,128)(2,1)S(1)}, bf16[8,289,289]{2,0,1:T(8,128)(2,1)}, u32[]{:S(2)}) copy-start(bf16[8,289,289]{2,0,1:T(8,128)(2,1)} %param.10) | copy-start | bytes 4009012
  6.9 26.4 %copy-start.11 = (s32[1,1,64,16]{2,3,1,0:T(8,128)S(1)}, s32[1,1,64,16]{2,3,1,0:T(8,128)}, u32[]{:S(2)}) copy-start(s32[1,1,64,16]{2,3,1,0:T(8,128)} %param.13) | copy-start | bytes 12292
  10.0 68.3 %all-to-all-start = ((bf16[512,289,1]{1,2,0:T(2,128)(2,1)}), bf16[512,289,1]{1,2,0:T(2,128)(2,1)S(1)}, u32[]{:S(2)}, u32[]{:S(2)}) async-start(bf16[512,289,1]{1,2,0:T(2,128)(2,1)} %stack.2), calls=%async_computation | async-start | bytes 1572864 | tf_op jit(solution)/shard_map/all_to_all | solution.py:51
  33.5 5.1 %copy-start.12 = (s32[8,64]{1,0:T(8,128)S(1)}, s32[8,64]{1,0:T(8,128)}, u32[]{:S(2)}) copy-start(s32[8,64]{1,0:T(8,128)} %param.17) | copy-start | bytes 6148
  33.5 5.3 %copy-start.13 = (s32[8,64]{1,0:T(8,128)S(1)}, s32[8,64]{1,0:T(8,128)}, u32[]{:S(2)}) copy-start(s32[8,64]{1,0:T(8,128)} %param.16) | copy-start | bytes 6148
  33.5 5.5 %copy-start.9 = (s32[16,512]{1,0:T(8,128)S(1)}, s32[16,512]{1,0:T(8,128)}, u32[]{:S(2)}) copy-start(s32[16,512]{1,0:T(8,128)} %param.14) | copy-start | bytes 98308
  38.5 46.2 %copy-start.3 = (bf16[8,289,289]{2,0,1:T(8,128)(2,1)S(1)}, bf16[8,289,289]{2,0,1:T(8,128)(2,1)}, u32[]{:S(2)}) copy-start(bf16[8,289,289]{2,0,1:T(8,128)(2,1)} %param.11) | copy-start | bytes 4009012
  78.3 49.7 %all-to-all-start.1 = ((bf16[289,64,16]{0,2,1:T(8,128)(2,1)}), bf16[289,64,16]{0,2,1:T(8,128)(2,1)}, u32[]{:S(2)}, u32[]{:S(2)}) async-start(bf16[289,64,16]{0,2,1:T(8,128)(2,1)} %broadcast_select_fusion), calls=%async_computation.1 | async-start | bytes 1572864 | tf_op jit(solution)/shard_map/all_to_all | solution.py:46
  87.9 4.2 %copy-start.10 = (s32[16,512]{1,0:T(8,128)S(1)}, s32[16,512]{1,0:T(8,128)}, u32[]{:S(2)}) copy-start(s32[16,512]{1,0:T(8,128)} %param.15) | copy-start | bytes 98308
  87.9 5.2 %copy-start = (bf16[8,289,289]{2,0,1:T(8,128)(2,1)S(1)}, bf16[8,289,289]{2,0,1:T(8,128)(2,1)}, u32[]{:S(2)}) copy-start(bf16[8,289,289]{2,0,1:T(8,128)(2,1)} %param.12) | copy-start | bytes 4009012
  105.3 3.2 %copy-start.6 = (bf16[8,289,289]{2,0,1:T(8,128)(2,1)S(1)}, bf16[8,289,289]{2,0,1:T(8,128)(2,1)}, u32[]{:S(2)}) copy-start(bf16[8,289,289]{2,0,1:T(8,128)(2,1)} %param.10) | copy-start | bytes 4009012
  109.8 2.6 %copy-start.4 = (bf16[8,289,289]{2,0,1:T(8,128)(2,1)S(1)}, bf16[8,289,289]{2,0,1:T(8,128)(2,1)}, u32[]{:S(2)}) copy-start(bf16[8,289,289]{2,0,1:T(8,128)(2,1)} %param.11) | copy-start | bytes 4009012
  109.9 3.2 %copy-start.2 = (bf16[2312,289]{0,1:T(8,128)(2,1)S(1)}, bf16[2312,289]{0,1:T(8,128)(2,1)}, u32[]{:S(2)}) copy-start(bf16[2312,289]{0,1:T(8,128)(2,1)} %reshape.142) | copy-start | bytes 4009012
  129.3 33.2 %copy-start.8 = (s32[16,512]{0,1:T(8,128)S(1)}, s32[16,512]{0,1:T(8,128)}, u32[]{:S(2)}) copy-start(s32[16,512]{0,1:T(8,128)} %copy.76) | copy-start | bytes 98308
  172.5 6.5 %copy-start.7 = (bf16[289,8,289]{0,1,2:T(8,128)(2,1)S(1)}, bf16[289,8,289]{0,1,2:T(8,128)(2,1)}, u32[]{:S(2)}) copy-start(bf16[289,8,289]{0,1,2:T(8,128)(2,1)} %copy.94) | copy-start | bytes 4009012
  179.0 3.8 %copy-start.1 = (f32[512,8,289]{0,1,2:T(8,128)S(1)}, f32[512,8,289]{0,1,2:T(8,128)}, u32[]{:S(2)}) copy-start(f32[512,8,289]{0,1,2:T(8,128)} %copy.83) | copy-start | bytes 14204932
